TPU v7x, 128 devices: a whole 4x4x4 slice. The times are simulated.
128 devices in a mesh: req: 8 (over y, core), voc: 16 (over x, z).
Axes of the slice: x: 4, y: 4, z: 4, core: 2. Of those that a mesh axis runs over, the one named last changes fastest.
Arguments:
- hidden: bfloat16 [16384, 1536], P(('req', 'voc')), may hold values from -64 to 64
- norm_gain: float32 [1536], replicated, may hold values from 0.1 to 1.9
- head: bfloat16 [1536, 49152], P(None, 'voc'), may hold values from -8 to 8
- targets: int32 [16384], P(('req', 'voc')), may hold values from 0 to 49151
- bounds: int32 [128, 2], P(('req', 'voc')), may hold values from 0 to 128, as said below
Outputs:
- logprob: float32 [16384], P(('req', 'voc'))
- entropy: float32 [16384], P(('req', 'voc'))
- target_logit: float32 [16384], P(('req', 'voc'))
- mean_entropy: float32 [1], replicated
Inputs may be any that keep to these rules, and one draw needn't show every extreme that they name: bounds[d] = (lo, hi): slots lo to hi - 1 of device d hold live response rows; 1 <= hi - lo <= 96, lo <= 32; some device has hi - lo = 96 and hi = 128, some has lo = 0.
All inputs are finite; a program needn't handle non-finite values.
Results may differ from a plain program's by a relative error of at most 0.00075.
The roundings to bfloat16 on the way count: a program that leaves them out, or rounds other values in their place, can miss the bound.
Values may be sent and summed in bfloat16 or wider, within the bound.
No kernel may reach another device: no remote copies, remote signals or barrier semaphores. Data moves between devices by JAX's collectives and lax.ppermute only.
A program may use at most 64 MiB of HBM per device.

v0:
```python
import jax
import jax.numpy as jnp
from jax import lax
from jax.sharding import PartitionSpec as P


def joined(part, axis, combine):
    gathered = jax.tree.map(lambda a: lax.all_gather(a, axis), part)

    def take(source):
        return jax.tree.map(lambda a: lax.dynamic_index_in_dim(a, source, 0, False), gathered)

    return lax.fori_loop(
        1, lax.axis_size(axis), lambda source, state: combine(state, take(source)), take(0)
    )


def pick_block(count):
    size = min(count, 512)
    while count % size:
        size -= 1
    return size


def combine_stats(first, second):
    top = jnp.maximum(first[0], second[0])
    weight_a = jnp.exp(first[0] - top)
    weight_b = jnp.exp(second[0] - top)
    return (
        top,
        first[1] * weight_a + second[1] * weight_b,
        first[2] * weight_a + second[2] * weight_b,
        first[3] + second[3],
    )


def shard_stats(gathered, local_ids, head):
    count = gathered.shape[0]
    width = gathered.shape[1]
    block = pick_block(count)
    columns = jnp.arange(head.shape[1], dtype=jnp.int32)

    def one_block(pair):
        rows_in, ids = pair
        logits = jnp.dot(rows_in, head, preferred_element_type=jnp.float32)
        top = jnp.max(logits, axis=-1)
        expo = jnp.exp(logits - top[:, None])
        total = jnp.sum(expo, axis=-1)
        weighted = jnp.sum(expo * logits, axis=-1)
        picked = jnp.sum(jnp.where(columns[None, :] == ids[:, None], logits, 0.0), axis=-1)
        return (top, total, weighted, picked)

    outputs = lax.map(
        one_block,
        (gathered.reshape(count // block, block, width), local_ids.reshape(count // block, block)),
    )
    return tuple((a.reshape(count) for a in outputs))


def shards(hidden, norm_gain, head, targets, bounds):
    slots = hidden.shape[0]
    shard_width = head.shape[1]
    position = lax.axis_index("voc")
    values = hidden.astype(jnp.float32)
    meansq = jnp.mean(values * values, axis=-1, keepdims=True)
    normed = (values * lax.rsqrt(meansq + 1e-05) * norm_gain).astype(jnp.bfloat16)
    start = bounds[0, 0]
    finish = bounds[0, 1]
    gathered, gathered_ids = (
        lax.all_gather(normed, "voc", axis=0, tiled=True),
        lax.all_gather(targets, "voc", axis=0, tiled=True),
    )
    local_ids = gathered_ids - position * shard_width
    stats = shard_stats(gathered, local_ids, head)
    merged = joined(stats, "voc", combine_stats)
    top, total, weighted, picked = [
        lax.dynamic_slice_in_dim(a, position * slots, slots, 0) for a in merged
    ]
    lse = top + jnp.log(total)
    row_entropy = lse - weighted / total
    row_logprob = picked - lse
    slot_index = jnp.arange(slots, dtype=jnp.int32)
    live = (slot_index >= start) & (slot_index < finish)
    zero = jnp.zeros((slots,), jnp.float32)
    entropy = jnp.where(live, row_entropy, zero)
    logprob = jnp.where(live, row_logprob, zero)
    target_logit = jnp.where(live, picked, zero)
    ent_sum, live_count = lax.psum(
        (jnp.sum(entropy), jnp.sum(live.astype(jnp.float32))), ("req", "voc")
    )
    mean_entropy = (ent_sum / live_count).reshape(1)
    return (logprob, entropy, target_logit, mean_entropy)


def solution(mesh):
    placed = (
        P(("req", "voc"), None),
        P(),
        P(None, "voc"),
        P(("req", "voc")),
        P(("req", "voc"), None),
    )
    return jax.shard_map(
        shards,
        mesh=mesh,
        in_specs=placed,
        out_specs=(P(("req", "voc")), P(("req", "voc")), P(("req", "voc")), P()),
        check_vma=False,
    )
```

profile of v0, /device:TPU:1, one launch (start us, length us, event | category | flops | bytes accessed | tf_op | source)
XLA Modules:
  0.0 286.2 jit_solution(3310339040187960190)
XLA Ops:
  7.2 0.0 all-gather.7.cloned.1.call-start
  7.2 1.2 fusion.7
  8.4 1.9 fusion.9
  10.3 0.0 all-gather.7.cloned.1.call-update
  10.4 18.7 %all-gather = s32[16,1,128]{2,1,0:T(1,128)S(1)} all-gather(s32[1,1,128]{2,1,0:T(1,128)} %bitcast.76), channel_id=1, replica_groups=mesh['req'=8,'voc'=16] {'voc'}, dimensions={0}, use_global_device_ids=true | all-gather | bytes 8704 | tf_op jit(solution)/shard_map/all_gather | solution.py:71
  29.1 1.3 fusion.12
  30.5 2.0 convert_reduce_fusion
  32.4 42.5 %all-gather.7.cloned.1.call-done = bf16[2048,1536]{1,0:T(8,128)(2,1)} async-done(((bf16[128,1536]{1,0:T(8,128)(2,1)}), bf16[2048,1536]{1,0:T(8,128)(2,1)}) %all-gather.7.cloned.1.call-update) | async-done | bytes 6291472 | tf_op jit(solution)/shard_map/all_gather | solution.py:70
  74.9 44.3 %while.39 = (s32[]{:T(128)}, f32[4,512]{1,0:T(4,128)S(1)}, f32[4,512]{1,0:T(4,128)S(1)}, f32[4,512]{1,0:T(4,128)S(1)}, f32[4,512]{1,0:T(4,128)S(1)}, /*index=5*/...) while((s32[]{:T(128)}, f32[4,512]{1,0:T(4,128)S(1)}, ...), condition=%wide.region_6.7_spmd.clone, body=%wide.region_1.6_spmd.clone.sunk | while | flops 4844419072 | bytes 23626360 | solution.py:53
  74.9 8.2 %fusion.17 = (f32[512]{0:T(512)S(1)}, f32[512,3072]{1,0:T(8,128)S(1)}) fusion(bf16[1536,3072]{1,0:T(8,128)(2,1)} %get-tuple-element.510, bf16[4,512,1536]{2,1,0:T(8,128)(2,1)} %get-tuple-element.509, s32[]{:T(128)} %get-tuple-element.494), kind=kOutput, calls=%fused_computation.37.clone.1 | convolution fusion | flops 4833410560 | bytes 17304064 | tf_op jit(solution)/shard_map/while/body/eval_jaxpr/dot_general | solution.py:45
  83.2 2.6 multiply_reduce_fusion.2
  85.8 0.1 dynamic_update_slice.24
  85.9 0.1 dynamic_update_slice.22
  85.9 0.1 dynamic_update_slice.21
  86.0 8.2 %fusion.17 = (f32[512]{0:T(512)S(1)}, f32[512,3072]{1,0:T(8,128)S(1)}) fusion(bf16[1536,3072]{1,0:T(8,128)(2,1)} %get-tuple-element.510, bf16[4,512,1536]{2,1,0:T(8,128)(2,1)} %get-tuple-element.509, s32[]{:T(128)} %get-tuple-element.494), kind=kOutput, calls=%fused_computation.37.clone.1 | convolution fusion | flops 4833410560 | bytes 17304064 | tf_op jit(solution)/shard_map/while/body/eval_jaxpr/dot_general | solution.py:45
  94.3 2.6 multiply_reduce_fusion.2
  96.9 0.1 dynamic_update_slice.24
  97.0 0.1 dynamic_update_slice.22
  97.0 0.1 dynamic_update_slice.21
  97.1 8.2 %fusion.17 = (f32[512]{0:T(512)S(1)}, f32[512,3072]{1,0:T(8,128)S(1)}) fusion(bf16[1536,3072]{1,0:T(8,128)(2,1)} %get-tuple-element.510, bf16[4,512,1536]{2,1,0:T(8,128)(2,1)} %get-tuple-element.509, s32[]{:T(128)} %get-tuple-element.494), kind=kOutput, calls=%fused_computation.37.clone.1 | convolution fusion | flops 4833410560 | bytes 17304064 | tf_op jit(solution)/shard_map/while/body/eval_jaxpr/dot_general | solution.py:45
  105.4 2.6 multiply_reduce_fusion.2
  108.0 0.1 dynamic_update_slice.24
  108.1 0.1 dynamic_update_slice.22
  108.1 0.1 dynamic_update_slice.21
  108.2 8.2 %fusion.17 = (f32[512]{0:T(512)S(1)}, f32[512,3072]{1,0:T(8,128)S(1)}) fusion(bf16[1536,3072]{1,0:T(8,128)(2,1)} %get-tuple-element.510, bf16[4,512,1536]{2,1,0:T(8,128)(2,1)} %get-tuple-element.509, s32[]{:T(128)} %get-tuple-element.494), kind=kOutput, calls=%fused_computation.37.clone.1 | convolution fusion | flops 4833410560 | bytes 17304064 | tf_op jit(solution)/shard_map/while/body/eval_jaxpr/dot_general | solution.py:45
  116.5 2.6 multiply_reduce_fusion.2
  119.1 0.1 dynamic_update_slice.24
  119.2 0.1 dynamic_update_slice.22
  119.2 0.1 dynamic_update_slice.21
  119.3 18.0 %all-gather.3 = f32[16,1,2048]{2,1,0:T(1,128)S(1)} all-gather(f32[1,1,2048]{2,1,0:T(1,128)S(1)} %reshape.39), channel_id=1, replica_groups=mesh['req'=8,'voc'=16] {'voc'}, dimensions={0}, use_global_device_ids=true | all-gather | bytes 139264 | tf_op jit(solution)/shard_map/all_gather | solution.py:8
  137.4 16.5 %all-gather.4 = f32[16,1,2048]{2,1,0:T(1,128)S(1)} all-gather(f32[1,1,2048]{2,1,0:T(1,128)S(1)} %reshape.41), channel_id=1, replica_groups=mesh['req'=8,'voc'=16] {'voc'}, dimensions={0}, use_global_device_ids=true | all-gather | bytes 139264 | tf_op jit(solution)/shard_map/all_gather | solution.py:8
  154.0 17.0 %all-gather.1 = f32[16,1,2048]{2,1,0:T(1,128)S(1)} all-gather(f32[1,1,2048]{2,1,0:T(1,128)S(1)} %reshape.35), channel_id=1, replica_groups=mesh['req'=8,'voc'=16] {'voc'}, dimensions={0}, use_global_device_ids=true | all-gather | bytes 139264 | tf_op jit(solution)/shard_map/all_gather | solution.py:8
  171.2 16.8 %all-gather.2 = f32[16,1,2048]{2,1,0:T(1,128)S(1)} all-gather(f32[1,1,2048]{2,1,0:T(1,128)S(1)} %reshape.37), channel_id=1, replica_groups=mesh['req'=8,'voc'=16] {'voc'}, dimensions={0}, use_global_device_ids=true | all-gather | bytes 139264 | tf_op jit(solution)/shard_map/all_gather | solution.py:8
  188.0 2.1 while.38
  190.1 1.2 fusion.10
  191.3 85.5 %all-reduce = (f32[]{:T(128)}, f32[]{:T(128)}) all-reduce(f32[]{:T(128)} %get-tuple-element.346, f32[]{:T(128)} %get-tuple-element.344), channel_id=1, replica_groups=mesh['req'=8,'voc'=16] {'req','voc'}, use_global_device_ids=true, to_apply=%region_10.11 | all-reduce | flops 2 | bytes 16 | tf_op jit(solution)/shard_map/psum | solution.py:88
  (117 shorter events, 1.7 us)
Async XLA Ops:
  7.2 67.8 %all-gather.7.cloned.1.call-start = ((), (), s32[]{:S(2)}) async-start(), calls=%async_computation | async-start | bytes 6684672 | tf_op jit(solution)/shard_map/all_gather | solution.py:70
Sparse Core Ops, SparseCore 0:
  10.5 64.4 all-gather.6
where the time goes:
time: 287 us; the launch traced here: 286 us
  blocking collectives  173 us (60%)
  waiting for transfers between devices  42.5 us (15%)
  matrix products  32.9 us (11%)
  other arithmetic  17.2 us (6%)
  between operations  16.7 us (6%)
  local copies, waits for them, and re-layouts  3.1 us (1%)
    psum x1, blocking collectives, shards(): lax.psum((jnp.sum(entropy), jnp.sum(live.astype(jnp.float32))), ('req', '...  85.5 us
    all_gather x4, blocking collectives, joined(): gathered = jax.tree.map(lambda a: lax.all_gather(a, axis), part)  68.4 us
    all_gather x1, waiting for transfers between devices, shards(): lax.all_gather(normed, 'voc', axis=0, tiled=True)  42.5 us
    dot_general x4, matrix products, one_block(): logits = jnp.dot(rows_in, head, preferred_element_type=jnp.float32)  32.9 us
    all_gather x1, blocking collectives, shards(): lax.all_gather(targets, 'voc', axis=0, tiled=True)  18.7 us
    reduce_sum x4, other arithmetic, one_block(): weighted = jnp.sum(expo * logits, axis=-1)  10.4 us
  transfers between devices with their start and end apart: 1, of which 1 were waited for; matrix products, arithmetic and copies ran while one was open for 1% of the time, Pallas kernels for 0%

commit v1 on v0

--- a/solution.py
+++ b/solution.py
@@ -1,7 +1,40 @@
+import functools
 import jax
 import jax.numpy as jnp
 from jax import lax
 from jax.sharding import PartitionSpec as P
+
+
+def tasks_show(sample, pos_dim):
+    lower = jax.lax.axis_size("voc")
+    tmp, carry_in, z_new = (lower, jax.lax.axis_index("voc"), sample.shape[pos_dim])
+    samples = []
+    for s, hop_no in enumerate(sample.shape):
+        samples.append(hop_no * tmp if s == pos_dim else hop_no)
+    opened = lax.dynamic_update_slice_in_dim(
+        jnp.zeros(samples, sample.dtype), sample, carry_in * z_new, axis=pos_dim
+    )
+    y2 = inter = sample
+    for ix in [*range(1, tmp // 2 + 1)]:
+        rows = []
+        for s in tuple(range(tmp)):
+            rows.append((s, (s + 1) % tmp))
+        y2 = jax.lax.ppermute(y2, "voc", rows)
+        opened = lax.dynamic_update_slice_in_dim(
+            opened, y2, (carry_in - ix) % tmp * z_new, axis=pos_dim
+        )
+        if 2 * ix < tmp:
+            pile = []
+            for s in tuple(range(tmp)):
+                pile.append((s, (s - 1) % tmp))
+            inter = jax.lax.ppermute(inter, "voc", pile)
+            opened = lax.dynamic_update_slice_in_dim(
+                opened, inter, (carry_in + ix) % tmp * z_new, axis=pos_dim
+            )
+    return opened
+
+
+solve_outputs = functools.partial(tasks_show, pos_dim=0)
 
 
 def joined(part, axis, combine):
@@ -67,7 +100,7 @@
     start = bounds[0, 0]
     finish = bounds[0, 1]
     gathered, gathered_ids = (
-        lax.all_gather(normed, "voc", axis=0, tiled=True),
+        solve_outputs(normed),
         lax.all_gather(targets, "voc", axis=0, tiled=True),
     )
     local_ids = gathered_ids - position * shard_width

time: 287 us -> 330 us (1.15)
  starting transfers between devices: 0.04 us -> 36.7 us
  local copies, waits for them, and re-layouts: 3.1 us -> 17.2 us
  between operations: 16.7 us -> 3.31 us
  blocking collectives: 173 us -> 182 us
    all_gather x1 -> x0, waiting for transfers between devices: 42.5 us -> none  [shards(): lax.all_gather(normed, 'voc', axis=0, tiled=True)]
    ppermute x0 -> x15, waiting for transfers between devices: none -> 40.1 us  [the longest x8 39.5 us: tasks_show(): y2 = jax.lax.ppermute(y2, 'voc', rows)]
    ppermute x0 -> x15, starting transfers between devices: none -> 36.7 us  [the longest x7 34.2 us: tasks_show(): inter = jax.lax.ppermute(inter, 'voc', pile)]
    dynamic_update_slice x0 -> x15, local copies, waits for them, and re-layouts: none -> 11.8 us  [the longest x8 6.25 us: tasks_show(): lax.dynamic_update_slice_in_dim(opened, y2, (carry_in - ix) % tmp * z_new...]
    psum x1, blocking collectives: 85.5 us -> 96.4 us  [shards(): lax.psum((jnp.sum(entropy), jnp.sum(live.astype(jnp.float32))), ('req', '...]
  transfers between devices with their start and end apart: 1 -> 15, of which waited for: 1 -> 9; matrix products, arithmetic and copies ran while one was open for 1% -> 4% of each run, Pallas kernels for 0% -> 0%
where the time goes in v1:
time: 330 us
  blocking collectives  182 us (55%)
  waiting for transfers between devices  40.1 us (12%)
  starting transfers between devices  36.7 us (11%)
  matrix products  32.9 us (10%)
  local copies, waits for them, and re-layouts  17.2 us (5%)
  other arithmetic  16.1 us (5%)
  between operations  3.31 us (1%)
    psum x1, blocking collectives, shards(): lax.psum((jnp.sum(entropy), jnp.sum(live.astype(jnp.float32))), ('req', '...  96.4 us
    all_gather x4, blocking collectives, joined(): gathered = jax.tree.map(lambda a: lax.all_gather(a, axis), part)  67.2 us
    ppermute x8, waiting for transfers between devices, tasks_show(): y2 = jax.lax.ppermute(y2, 'voc', rows)  39.5 us
    ppermute x7, starting transfers between devices, tasks_show(): inter = jax.lax.ppermute(inter, 'voc', pile)  34.2 us
    dot_general x4, matrix products, one_block(): logits = jnp.dot(rows_in, head, preferred_element_type=jnp.float32)  32.9 us
    all_gather x1, blocking collectives, shards(): lax.all_gather(targets, 'voc', axis=0, tiled=True)  18.9 us
    reduce_sum x4, other arithmetic, one_block(): weighted = jnp.sum(expo * logits, axis=-1)  10.4 us
  transfers between devices with their start and end apart: 15, of which 9 were waited for; matrix products, arithmetic and copies ran while one was open for 4% of the time, Pallas kernels for 0%

profile of v1, /device:TPU:1, one launch (start us, length us, event | category | flops | bytes accessed | tf_op | source)
XLA Modules:
  0.0 329.8 jit_solution(3257770971862297256)
XLA Ops:
  0.7 1.2 fusion.7
  1.9 3.1 broadcast_in_dim.28
  5.0 0.9 constant_dynamic-update-slice_fusion.15
  5.9 2.5 collective-permute-start
  8.3 4.3 %collective-permute-start.1 = (bf16[128,1536]{1,0:T(8,128)(2,1)S(1)}, bf16[128,1536]{1,0:T(8,128)(2,1)S(1)}, u32[]{:S(2)}, u32[]{:S(2)}) collective-permute-start(bf16[128,1536]{1,0:T(8,128)(2,1)S(1)} %get-tuple-element.349), channel_id=1, source_target_pairs={{0,15},{1,0},{2,1},{3,2},{4,3},{5,4},{6,5},{7,6},{8,7},{9,8},{10,9... | collective-permute-start | bytes 1179656 | tf_op jit(solution)/shard_map/ppermute | solution.py:30
  12.6 18.9 %all-gather = s32[16,1,128]{2,1,0:T(1,128)S(1)} all-gather(s32[1,1,128]{2,1,0:T(1,128)S(1)} %bitcast.76), channel_id=1, replica_groups=mesh['req'=8,'voc'=16] {'voc'}, dimensions={0}, use_global_device_ids=true | all-gather | bytes 8704 | tf_op jit(solution)/shard_map/all_gather | solution.py:104
  32.3 2.0 convert_reduce_fusion
  34.2 4.8 %collective-permute-start.3 = (bf16[128,1536]{1,0:T(8,128)(2,1)S(1)}, bf16[128,1536]{1,0:T(8,128)(2,1)S(1)}, u32[]{:S(2)}, u32[]{:S(2)}) collective-permute-start(bf16[128,1536]{1,0:T(8,128)(2,1)S(1)} %collective-permute-done.1), channel_id=1, source_target_pairs={{0,15},{1,0},{2,1},{3,2},{4,3},{5,4},{6,5},{7,6},{8,7},{9,8},{10,9... | collective-permute-start | bytes 1179656 | tf_op jit(solution)/shard_map/ppermute | solution.py:30
  39.8 0.8 constant_dynamic-update-slice_fusion.13
  40.6 3.6 %collective-permute-done.2 = bf16[128,1536]{1,0:T(8,128)(2,1)S(1)} collective-permute-done((bf16[128,1536]{1,0:T(8,128)(2,1)S(1)}, bf16[128,1536]{1,0:T(8,128)(2,1)S(1)}, u32[]{:S(2)}, u32[]{:S(2)}) %collective-permute-start.2) | collective-permute-done | bytes 393248 | tf_op jit(solution)/shard_map/ppermute | solution.py:22
  44.2 4.8 %collective-permute-start.5 = (bf16[128,1536]{1,0:T(8,128)(2,1)S(1)}, bf16[128,1536]{1,0:T(8,128)(2,1)S(1)}, u32[]{:S(2)}, u32[]{:S(2)}) collective-permute-start(bf16[128,1536]{1,0:T(8,128)(2,1)S(1)} %collective-permute-done.3), channel_id=1, source_target_pairs={{0,15},{1,0},{2,1},{3,2},{4,3},{5,4},{6,5},{7,6},{8,7},{9,8},{10,9... | collective-permute-start | bytes 1179656 | tf_op jit(solution)/shard_map/ppermute | solution.py:30
  49.0 0.8 constant_dynamic-update-slice_fusion.12
  49.8 0.8 constant_dynamic-update-slice_fusion.11
  50.6 3.6 %collective-permute-done.4 = bf16[128,1536]{1,0:T(8,128)(2,1)S(1)} collective-permute-done((bf16[128,1536]{1,0:T(8,128)(2,1)S(1)}, bf16[128,1536]{1,0:T(8,128)(2,1)S(1)}, u32[]{:S(2)}, u32[]{:S(2)}) %collective-permute-start.4) | collective-permute-done | bytes 393248 | tf_op jit(solution)/shard_map/ppermute | solution.py:22
  54.1 4.8 %collective-permute-start.7 = (bf16[128,1536]{1,0:T(8,128)(2,1)S(1)}, bf16[128,1536]{1,0:T(8,128)(2,1)S(1)}, u32[]{:S(2)}, u32[]{:S(2)}) collective-permute-start(bf16[128,1536]{1,0:T(8,128)(2,1)S(1)} %collective-permute-done.5), channel_id=1, source_target_pairs={{0,15},{1,0},{2,1},{3,2},{4,3},{5,4},{6,5},{7,6},{8,7},{9,8},{10,9... | collective-permute-start | bytes 1179656 | tf_op jit(solution)/shard_map/ppermute | solution.py:30
  58.9 0.8 constant_dynamic-update-slice_fusion.10
  59.7 0.8 constant_dynamic-update-slice_fusion.9
  60.5 3.7 %collective-permute-done.6 = bf16[128,1536]{1,0:T(8,128)(2,1)S(1)} collective-permute-done((bf16[128,1536]{1,0:T(8,128)(2,1)S(1)}, bf16[128,1536]{1,0:T(8,128)(2,1)S(1)}, u32[]{:S(2)}, u32[]{:S(2)}) %collective-permute-start.6) | collective-permute-done | bytes 393248 | tf_op jit(solution)/shard_map/ppermute | solution.py:22
  64.2 5.1 %collective-permute-start.9 = (bf16[128,1536]{1,0:T(8,128)(2,1)S(1)}, bf16[128,1536]{1,0:T(8,128)(2,1)S(1)}, u32[]{:S(2)}, u32[]{:S(2)}) collective-permute-start(bf16[128,1536]{1,0:T(8,128)(2,1)S(1)} %collective-permute-done.7), channel_id=1, source_target_pairs={{0,15},{1,0},{2,1},{3,2},{4,3},{5,4},{6,5},{7,6},{8,7},{9,8},{10,9... | collective-permute-start | bytes 1179656 | tf_op jit(solution)/shard_map/ppermute | solution.py:30
  69.2 0.8 constant_dynamic-update-slice_fusion.8
  70.0 0.8 constant_dynamic-update-slice_fusion.7
  70.8 4.6 %collective-permute-done.8 = bf16[128,1536]{1,0:T(8,128)(2,1)S(1)} collective-permute-done((bf16[128,1536]{1,0:T(8,128)(2,1)S(1)}, bf16[128,1536]{1,0:T(8,128)(2,1)S(1)}, u32[]{:S(2)}, u32[]{:S(2)}) %collective-permute-start.8) | collective-permute-done | bytes 393248 | tf_op jit(solution)/shard_map/ppermute | solution.py:22
  75.5 5.2 %collective-permute-start.11 = (bf16[128,1536]{1,0:T(8,128)(2,1)S(1)}, bf16[128,1536]{1,0:T(8,128)(2,1)S(1)}, u32[]{:S(2)}, u32[]{:S(2)}) collective-permute-start(bf16[128,1536]{1,0:T(8,128)(2,1)S(1)} %collective-permute-done.9), channel_id=1, source_target_pairs={{0,15},{1,0},{2,1},{3,2},{4,3},{5,4},{6,5},{7,6},{8,7},{9,8},{10,9... | collective-permute-start | bytes 1179656 | tf_op jit(solution)/shard_map/ppermute | solution.py:30
  80.7 0.8 constant_dynamic-update-slice_fusion.6
  81.5 0.8 constant_dynamic-update-slice_fusion.5
  82.3 5.4 %collective-permute-done.10 = bf16[128,1536]{1,0:T(8,128)(2,1)S(1)} collective-permute-done((bf16[128,1536]{1,0:T(8,128)(2,1)S(1)}, bf16[128,1536]{1,0:T(8,128)(2,1)S(1)}, u32[]{:S(2)}, u32[]{:S(2)}) %collective-permute-start.10) | collective-permute-done | bytes 393248 | tf_op jit(solution)/shard_map/ppermute | solution.py:22
  88.1 5.2 %collective-permute-start.13 = (bf16[128,1536]{1,0:T(8,128)(2,1)S(1)}, bf16[128,1536]{1,0:T(8,128)(2,1)S(1)}, u32[]{:S(2)}, u32[]{:S(2)}) collective-permute-start(bf16[128,1536]{1,0:T(8,128)(2,1)S(1)} %collective-permute-done.11), channel_id=1, source_target_pairs={{0,15},{1,0},{2,1},{3,2},{4,3},{5,4},{6,5},{7,6},{8,7},{9,8},{10,9... | collective-permute-start | bytes 1179656 | tf_op jit(solution)/shard_map/ppermute | solution.py:30
  94.1 0.8 constant_dynamic-update-slice_fusion.3
  94.9 6.3 %collective-permute-done.12 = bf16[128,1536]{1,0:T(8,128)(2,1)S(1)} collective-permute-done((bf16[128,1536]{1,0:T(8,128)(2,1)S(1)}, bf16[128,1536]{1,0:T(8,128)(2,1)S(1)}, u32[]{:S(2)}, u32[]{:S(2)}) %collective-permute-start.12) | collective-permute-done | bytes 393248 | tf_op jit(solution)/shard_map/ppermute | solution.py:22
  102.0 0.8 constant_dynamic-update-slice_fusion.1
  102.8 12.4 %collective-permute-done.14 = bf16[128,1536]{1,0:T(8,128)(2,1)S(1)} collective-permute-done((bf16[128,1536]{1,0:T(8,128)(2,1)S(1)}, bf16[128,1536]{1,0:T(8,128)(2,1)S(1)}, u32[]{:S(2)}, u32[]{:S(2)}) %collective-permute-start.14) | collective-permute-done | bytes 393248 | tf_op jit(solution)/shard_map/ppermute | solution.py:22
  115.2 0.8 constant_dynamic-update-slice_fusion
  115.9 44.3 %while.39 = (s32[]{:T(128)}, f32[4,512]{1,0:T(4,128)S(1)}, f32[4,512]{1,0:T(4,128)S(1)}, f32[4,512]{1,0:T(4,128)S(1)}, f32[4,512]{1,0:T(4,128)S(1)}, /*index=5*/...) while((s32[]{:T(128)}, f32[4,512]{1,0:T(4,128)S(1)}, ...), condition=%wide.region_6.7_spmd.clone, body=%wide.region_1.6_spmd.clone.sunk | while | flops 4844419072 | bytes 23626360 | solution.py:86
  115.9 8.2 %fusion.18 = (f32[512]{0:T(512)S(1)}, f32[512,3072]{1,0:T(8,128)S(1)}) fusion(bf16[1536,3072]{1,0:T(8,128)(2,1)} %get-tuple-element.512, bf16[4,512,1536]{2,1,0:T(8,128)(2,1)} %get-tuple-element.511, s32[]{:T(128)} %get-tuple-element.496), kind=kOutput, calls=%fused_computation.53.clone.1 | convolution fusion | flops 4833410560 | bytes 17304064 | tf_op jit(solution)/shard_map/while/body/eval_jaxpr/dot_general | solution.py:78
  124.2 2.6 multiply_reduce_fusion.2
  127.0 8.2 %fusion.18 = (f32[512]{0:T(512)S(1)}, f32[512,3072]{1,0:T(8,128)S(1)}) fusion(bf16[1536,3072]{1,0:T(8,128)(2,1)} %get-tuple-element.512, bf16[4,512,1536]{2,1,0:T(8,128)(2,1)} %get-tuple-element.511, s32[]{:T(128)} %get-tuple-element.496), kind=kOutput, calls=%fused_computation.53.clone.1 | convolution fusion | flops 4833410560 | bytes 17304064 | tf_op jit(solution)/shard_map/while/body/eval_jaxpr/dot_general | solution.py:78
  135.3 2.6 multiply_reduce_fusion.2
  138.1 8.2 %fusion.18 = (f32[512]{0:T(512)S(1)}, f32[512,3072]{1,0:T(8,128)S(1)}) fusion(bf16[1536,3072]{1,0:T(8,128)(2,1)} %get-tuple-element.512, bf16[4,512,1536]{2,1,0:T(8,128)(2,1)} %get-tuple-element.511, s32[]{:T(128)} %get-tuple-element.496), kind=kOutput, calls=%fused_computation.53.clone.1 | convolution fusion | flops 4833410560 | bytes 17304064 | tf_op jit(solution)/shard_map/while/body/eval_jaxpr/dot_general | solution.py:78
  146.4 2.6 multiply_reduce_fusion.2
  149.2 8.2 %fusion.18 = (f32[512]{0:T(512)S(1)}, f32[512,3072]{1,0:T(8,128)S(1)}) fusion(bf16[1536,3072]{1,0:T(8,128)(2,1)} %get-tuple-element.512, bf16[4,512,1536]{2,1,0:T(8,128)(2,1)} %get-tuple-element.511, s32[]{:T(128)} %get-tuple-element.496), kind=kOutput, calls=%fused_computation.53.clone.1 | convolution fusion | flops 4833410560 | bytes 17304064 | tf_op jit(solution)/shard_map/while/body/eval_jaxpr/dot_general | solution.py:78
  157.4 2.6 multiply_reduce_fusion.2
  160.3 15.5 %all-gather.3 = f32[16,1,2048]{2,1,0:T(1,128)S(1)} all-gather(f32[1,1,2048]{2,1,0:T(1,128)S(1)} %reshape.39), channel_id=1, replica_groups=mesh['req'=8,'voc'=16] {'voc'}, dimensions={0}, use_global_device_ids=true | all-gather | bytes 139264 | tf_op jit(solution)/shard_map/all_gather | solution.py:41
  175.8 18.1 %all-gather.4 = f32[16,1,2048]{2,1,0:T(1,128)S(1)} all-gather(f32[1,1,2048]{2,1,0:T(1,128)S(1)} %reshape.41), channel_id=1, replica_groups=mesh['req'=8,'voc'=16] {'voc'}, dimensions={0}, use_global_device_ids=true | all-gather | bytes 139264 | tf_op jit(solution)/shard_map/all_gather | solution.py:41
  194.0 16.1 %all-gather.1 = f32[16,1,2048]{2,1,0:T(1,128)S(1)} all-gather(f32[1,1,2048]{2,1,0:T(1,128)S(1)} %reshape.35), channel_id=1, replica_groups=mesh['req'=8,'voc'=16] {'voc'}, dimensions={0}, use_global_device_ids=true | all-gather | bytes 139264 | tf_op jit(solution)/shard_map/all_gather | solution.py:41
  210.2 17.5 %all-gather.2 = f32[16,1,2048]{2,1,0:T(1,128)S(1)} all-gather(f32[1,1,2048]{2,1,0:T(1,128)S(1)} %reshape.37), channel_id=1, replica_groups=mesh['req'=8,'voc'=16] {'voc'}, dimensions={0}, use_global_device_ids=true | all-gather | bytes 139264 | tf_op jit(solution)/shard_map/all_gather | solution.py:41
  227.7 2.1 while.38
  229.8 1.2 fusion.10
  231.1 96.4 %all-reduce = (f32[]{:T(128)}, f32[]{:T(128)}) all-reduce(f32[]{:T(128)} %get-tuple-element.346, f32[]{:T(128)} %get-tuple-element.344), channel_id=1, replica_groups=mesh['req'=8,'voc'=16] {'req','voc'}, use_global_device_ids=true, to_apply=%region_10.11 | all-reduce | flops 2 | bytes 16 | tf_op jit(solution)/shard_map/psum | solution.py:121
  (156 shorter events, 5.7 us)
Async XLA Ops:
  0.6 4.3 %copy-start = (bf16[128,1536]{1,0:T(8,128)(2,1)S(1)}, bf16[128,1536]{1,0:T(8,128)(2,1)}, u32[]{:S(2)}) copy-start(bf16[128,1536]{1,0:T(8,128)(2,1)} %param.9) | copy-start | bytes 1179652
  0.6 4.3 %copy-start.1 = (f32[1536]{0:T(1024)S(1)}, f32[1536]{0:T(1024)}, u32[]{:S(2)}) copy-start(f32[1536]{0:T(1024)} %param.10) | copy-start | bytes 18436
  0.7 12.0 %copy-start.3 = (s32[128]{0:T(128)S(1)}, s32[128]{0:T(128)}, u32[]{:S(2)}) copy-start(s32[128]{0:T(128)} %param.12) | copy-start | bytes 1540
  0.7 31.0 %copy-start.2 = (s32[1,2]{1,0:T(1,128)S(1)}, s32[1,2]{1,0:T(1,128)}, u32[]{:S(2)}) copy-start(s32[1,2]{1,0:T(1,128)} %param.13) | copy-start | bytes 28
  5.9 28.4 %collective-permute-start = (bf16[128,1536]{1,0:T(8,128)(2,1)S(1)}, bf16[128,1536]{1,0:T(8,128)(2,1)S(1)}, u32[]{:S(2)}, u32[]{:S(2)}) collective-permute-start(bf16[128,1536]{1,0:T(8,128)(2,1)S(1)} %get-tuple-element.349), channel_id=1, source_target_pairs={{0,1},{1,2},{2,3},{3,4},{4,5},{5,6},{6,7},{7,8},{8,9},{9,10},{10,1... | collective-permute-start | bytes 1179656 | tf_op jit(solution)/shard_map/ppermute | solution.py:22
  8.3 25.9 %collective-permute-start.1 = (bf16[128,1536]{1,0:T(8,128)(2,1)S(1)}, bf16[128,1536]{1,0:T(8,128)(2,1)S(1)}, u32[]{:S(2)}, u32[]{:S(2)}) collective-permute-start(bf16[128,1536]{1,0:T(8,128)(2,1)S(1)} %get-tuple-element.349), channel_id=1, source_target_pairs={{0,15},{1,0},{2,1},{3,2},{4,3},{5,4},{6,5},{7,6},{8,7},{9,8},{10,9... | collective-permute-start | bytes 1179656 | tf_op jit(solution)/shard_map/ppermute | solution.py:30
  34.2 9.9 %collective-permute-start.2 = (bf16[128,1536]{1,0:T(8,128)(2,1)S(1)}, bf16[128,1536]{1,0:T(8,128)(2,1)S(1)}, u32[]{:S(2)}, u32[]{:S(2)}) collective-permute-start(bf16[128,1536]{1,0:T(8,128)(2,1)S(1)} %collective-permute-done), channel_id=1, source_target_pairs={{0,1},{1,2},{2,3},{3,4},{4,5},{5,6},{6,7},{7,8},{8,9},{9,10},{10,1... | collective-permute-start | bytes 1179656 | tf_op jit(solution)/shard_map/ppermute | solution.py:22
  34.2 9.9 %collective-permute-start.3 = (bf16[128,1536]{1,0:T(8,128)(2,1)S(1)}, bf16[128,1536]{1,0:T(8,128)(2,1)S(1)}, u32[]{:S(2)}, u32[]{:S(2)}) collective-permute-start(bf16[128,1536]{1,0:T(8,128)(2,1)S(1)} %collective-permute-done.1), channel_id=1, source_target_pairs={{0,15},{1,0},{2,1},{3,2},{4,3},{5,4},{6,5},{7,6},{8,7},{9,8},{10,9... | collective-permute-start | bytes 1179656 | tf_op jit(solution)/shard_map/ppermute | solution.py:30
  44.2 9.9 %collective-permute-start.4 = (bf16[128,1536]{1,0:T(8,128)(2,1)S(1)}, bf16[128,1536]{1,0:T(8,128)(2,1)S(1)}, u32[]{:S(2)}, u32[]{:S(2)}) collective-permute-start(bf16[128,1536]{1,0:T(8,128)(2,1)S(1)} %collective-permute-done.2), channel_id=1, source_target_pairs={{0,1},{1,2},{2,3},{3,4},{4,5},{5,6},{6,7},{7,8},{8,9},{9,10},{10,1... | collective-permute-start | bytes 1179656 | tf_op jit(solution)/shard_map/ppermute | solution.py:22
  44.2 9.9 %collective-permute-start.5 = (bf16[128,1536]{1,0:T(8,128)(2,1)S(1)}, bf16[128,1536]{1,0:T(8,128)(2,1)S(1)}, u32[]{:S(2)}, u32[]{:S(2)}) collective-permute-start(bf16[128,1536]{1,0:T(8,128)(2,1)S(1)} %collective-permute-done.3), channel_id=1, source_target_pairs={{0,15},{1,0},{2,1},{3,2},{4,3},{5,4},{6,5},{7,6},{8,7},{9,8},{10,9... | collective-permute-start | bytes 1179656 | tf_op jit(solution)/shard_map/ppermute | solution.py:30
  54.1 10.0 %collective-permute-start.6 = (bf16[128,1536]{1,0:T(8,128)(2,1)S(1)}, bf16[128,1536]{1,0:T(8,128)(2,1)S(1)}, u32[]{:S(2)}, u32[]{:S(2)}) collective-permute-start(bf16[128,1536]{1,0:T(8,128)(2,1)S(1)} %collective-permute-done.4), channel_id=1, source_target_pairs={{0,1},{1,2},{2,3},{3,4},{4,5},{5,6},{6,7},{7,8},{8,9},{9,10},{10,1... | collective-permute-start | bytes 1179656 | tf_op jit(solution)/shard_map/ppermute | solution.py:22
  54.1 10.0 %collective-permute-start.7 = (bf16[128,1536]{1,0:T(8,128)(2,1)S(1)}, bf16[128,1536]{1,0:T(8,128)(2,1)S(1)}, u32[]{:S(2)}, u32[]{:S(2)}) collective-permute-start(bf16[128,1536]{1,0:T(8,128)(2,1)S(1)} %collective-permute-done.5), channel_id=1, source_target_pairs={{0,15},{1,0},{2,1},{3,2},{4,3},{5,4},{6,5},{7,6},{8,7},{9,8},{10,9... | collective-permute-start | bytes 1179656 | tf_op jit(solution)/shard_map/ppermute | solution.py:30
  64.2 11.2 %collective-permute-start.8 = (bf16[128,1536]{1,0:T(8,128)(2,1)S(1)}, bf16[128,1536]{1,0:T(8,128)(2,1)S(1)}, u32[]{:S(2)}, u32[]{:S(2)}) collective-permute-start(bf16[128,1536]{1,0:T(8,128)(2,1)S(1)} %collective-permute-done.6), channel_id=1, source_target_pairs={{0,1},{1,2},{2,3},{3,4},{4,5},{5,6},{6,7},{7,8},{8,9},{9,10},{10,1... | collective-permute-start | bytes 1179656 | tf_op jit(solution)/shard_map/ppermute | solution.py:22
  64.2 11.3 %collective-permute-start.9 = (bf16[128,1536]{1,0:T(8,128)(2,1)S(1)}, bf16[128,1536]{1,0:T(8,128)(2,1)S(1)}, u32[]{:S(2)}, u32[]{:S(2)}) collective-permute-start(bf16[128,1536]{1,0:T(8,128)(2,1)S(1)} %collective-permute-done.7), channel_id=1, source_target_pairs={{0,15},{1,0},{2,1},{3,2},{4,3},{5,4},{6,5},{7,6},{8,7},{9,8},{10,9... | collective-permute-start | bytes 1179656 | tf_op jit(solution)/shard_map/ppermute | solution.py:30
  75.4 12.3 %collective-permute-start.10 = (bf16[128,1536]{1,0:T(8,128)(2,1)S(1)}, bf16[128,1536]{1,0:T(8,128)(2,1)S(1)}, u32[]{:S(2)}, u32[]{:S(2)}) collective-permute-start(bf16[128,1536]{1,0:T(8,128)(2,1)S(1)} %collective-permute-done.8), channel_id=1, source_target_pairs={{0,1},{1,2},{2,3},{3,4},{4,5},{5,6},{6,7},{7,8},{8,9},{9,10},{10,1... | collective-permute-start | bytes 1179656 | tf_op jit(solution)/shard_map/ppermute | solution.py:22
  75.5 12.6 %collective-permute-start.11 = (bf16[128,1536]{1,0:T(8,128)(2,1)S(1)}, bf16[128,1536]{1,0:T(8,128)(2,1)S(1)}, u32[]{:S(2)}, u32[]{:S(2)}) collective-permute-start(bf16[128,1536]{1,0:T(8,128)(2,1)S(1)} %collective-permute-done.9), channel_id=1, source_target_pairs={{0,15},{1,0},{2,1},{3,2},{4,3},{5,4},{6,5},{7,6},{8,7},{9,8},{10,9... | collective-permute-start | bytes 1179656 | tf_op jit(solution)/shard_map/ppermute | solution.py:30
  87.7 13.5 %collective-permute-start.12 = (bf16[128,1536]{1,0:T(8,128)(2,1)S(1)}, bf16[128,1536]{1,0:T(8,128)(2,1)S(1)}, u32[]{:S(2)}, u32[]{:S(2)}) collective-permute-start(bf16[128,1536]{1,0:T(8,128)(2,1)S(1)} %collective-permute-done.10), channel_id=1, source_target_pairs={{0,1},{1,2},{2,3},{3,4},{4,5},{5,6},{6,7},{7,8},{8,9},{9,10},{10,1... | collective-permute-start | bytes 1179656 | tf_op jit(solution)/shard_map/ppermute | solution.py:22
  88.1 13.9 %collective-permute-start.13 = (bf16[128,1536]{1,0:T(8,128)(2,1)S(1)}, bf16[128,1536]{1,0:T(8,128)(2,1)S(1)}, u32[]{:S(2)}, u32[]{:S(2)}) collective-permute-start(bf16[128,1536]{1,0:T(8,128)(2,1)S(1)} %collective-permute-done.11), channel_id=1, source_target_pairs={{0,15},{1,0},{2,1},{3,2},{4,3},{5,4},{6,5},{7,6},{8,7},{9,8},{10,9... | collective-permute-start | bytes 1179656 | tf_op jit(solution)/shard_map/ppermute | solution.py:30
  101.2 14.0 %collective-permute-start.14 = (bf16[128,1536]{1,0:T(8,128)(2,1)S(1)}, bf16[128,1536]{1,0:T(8,128)(2,1)S(1)}, u32[]{:S(2)}, u32[]{:S(2)}) collective-permute-start(bf16[128,1536]{1,0:T(8,128)(2,1)S(1)} %collective-permute-done.12), channel_id=1, source_target_pairs={{0,1},{1,2},{2,3},{3,4},{4,5},{5,6},{6,7},{7,8},{8,9},{9,10},{10,1... | collective-permute-start | bytes 1179656 | tf_op jit(solution)/shard_map/ppermute | solution.py:22
